TPU v7x, 128 devices: a whole 4x4x4 slice. The times are simulated.
128 devices in a mesh: req: 16 (over z, x), mlp: 8 (over y, core).
Axes of the slice: x: 4, y: 4, z: 4, core: 2. Of those that a mesh axis runs over, the one named last changes fastest.
Arguments:
- residual_input: bfloat16 [9216, 5120], P('req', 'mlp'), as said below
- attention_output: bfloat16 [9216, 3072], P('req', 'mlp'), may hold values from -6 to 6
- request_length: int32 [16, 4], replicated, may hold values from 1 to 573, as said below
- request_group: int32 [64], replicated, may hold values from 0 to 7
- adapter_per_group: int32 [8], replicated, may hold values from 0 to 15
- output_weight: bfloat16 [3072, 5120], P('mlp', 'req'), may hold values from -0.109375 to 0.109375
- output_down_maps: bfloat16 [3072, 16, 16], P('mlp'), may hold values from -0.109375 to 0.109375
- output_up_maps: bfloat16 [16, 16, 5120], P(None, None, 'mlp'), may hold values from -1.5 to 1.5
- modulation: float32 [8, 3, 5120], replicated, may hold values from -3 to 3
- hidden_down_maps: bfloat16 [5120, 16, 16], P('mlp'), may hold values from -0.078125 to 0.078125
- hidden_up_maps: bfloat16 [16, 16, 6912], P(None, None, 'mlp'), may hold values from -1.5 to 1.5
- up_weight: bfloat16 [5120, 6912], P('req', 'mlp'), may hold values from -0.078125 to 0.078125
- down_weight: bfloat16 [6912, 5120], P('mlp', 'req'), may hold values from -0.078125 to 0.078125
Outputs:
- layer_out: bfloat16 [384, 16, 5120], P(None, 'req', 'mlp')
Inputs may be any that keep to these rules, and one draw needn't show every extreme that they name: `request_length`: the 4 lengths of one block sum to at most 576, and to exactly 576 for one block; all lengths together sum to 6144. One request has exactly the largest length. `residual_input`: rows of a block past its live rows are never read.
All inputs are finite; a program needn't handle non-finite values.
Results may differ from a plain program's by a relative error of at most 0.012.
Values may be sent and summed in bfloat16 or wider, within the bound.
No kernel may reach another device: no remote copies, remote signals or barrier semaphores. Data moves between devices by JAX's collectives and lax.ppermute only.
A program may use at most 192 MiB of HBM per device.

v0:
```python
import jax
import jax.numpy as jnp
from jax import lax
from jax.sharding import PartitionSpec as P

MODEL_WIDTH = 5120
ADAPTER_RANK = 16
ADAPTER_TOTAL = 16
TOK_DEV = 384
CAP = 576


norm_epsilon = 1e-06


def send_layout(packed, offset, req_count):
    shaped = packed.reshape(packed.shape[0] // req_count, req_count, packed.shape[1])
    return jnp.roll(shaped, offset, axis=1)


def compact(moved, starts, ends, req_count, device_index):
    slots = moved.shape[0] * moved.shape[1]
    flat_rows = moved.reshape(slots, moved.shape[2])
    token_rank = jnp.arange(TOK_DEV, dtype=jnp.int32) * req_count + device_index
    source = jnp.sum((ends[None, :] <= token_rank[:, None]).astype(jnp.int32), axis=1)
    source_hot = source[:, None] == jnp.arange(req_count, dtype=jnp.int32)[None, :]
    source_start = jnp.sum(jnp.where(source_hot, starts[None, :], 0), axis=1)
    position = (token_rank - source_start) // req_count * req_count + source
    return jnp.take(flat_rows, position, axis=0)


def token_tables(token_rank, request_length, request_group, adapter_per_group, modulation):
    req_ends = jnp.cumsum(request_length.reshape(-1))
    request_count = req_ends.shape[0]
    request = jnp.sum((req_ends[None, :] <= token_rank[:, None]).astype(jnp.int32), axis=1)
    request = jnp.minimum(request, request_count - 1)
    request_hot = request[:, None] == jnp.arange(request_count, dtype=jnp.int32)[None, :]
    group_ids = jnp.sum(jnp.where(request_hot, request_group[None, :], 0), axis=1)
    group_count = adapter_per_group.shape[0]
    group_hot = group_ids[:, None] == jnp.arange(group_count, dtype=jnp.int32)[None, :]
    adapter_of_row = jnp.sum(jnp.where(group_hot, adapter_per_group[None, :], 0), axis=1)
    adapter_hot = (
        adapter_of_row[:, None] == jnp.arange(ADAPTER_TOTAL, dtype=jnp.int32)[None, :]
    ).astype(jnp.float32)
    mod_rows = jnp.dot(
        group_hot.astype(jnp.float32),
        modulation.reshape(group_count, -1),
        precision=lax.Precision.HIGHEST,
    )
    return (adapter_hot, mod_rows.reshape(token_rank.shape[0], 3, modulation.shape[2]))


def select_low(output_rank_rows, adapter_hot):
    shaped = output_rank_rows.reshape(output_rank_rows.shape[0], ADAPTER_TOTAL, ADAPTER_RANK)
    return jnp.sum(shaped * adapter_hot[:, :, None], axis=1)


def expand_rank_rows(low_rows, adapter_hot):
    spread_rows = adapter_hot.astype(jnp.bfloat16)[:, :, None] * low_rows[:, None, :]
    return spread_rows.reshape(low_rows.shape[0], ADAPTER_TOTAL * ADAPTER_RANK)


def layer_rows(
    attention_rows,
    residual_rows,
    token_rank,
    request_length,
    request_group,
    adapter_per_group,
    output_weight,
    output_down_maps,
    output_up_maps,
    modulation,
    hidden_down_maps,
    hidden_up_maps,
    up_weight,
    down_weight,
):
    column_index = lax.axis_index("mlp")
    shard_hidden_width = residual_rows.shape[1]
    adapter_hot, mod_rows = token_tables(
        token_rank, request_length, request_group, adapter_per_group, modulation
    )
    shift_rows = mod_rows[:, 0]
    scale_rows = mod_rows[:, 1]
    gate_rows = lax.dynamic_slice_in_dim(
        mod_rows[:, 2], column_index * shard_hidden_width, shard_hidden_width, 1
    )
    head_terms = jnp.dot(
        attention_rows,
        lax.all_gather(output_weight, "req", axis=1, tiled=True),
        preferred_element_type=jnp.float32,
    )
    projection_rows = lax.psum_scatter(
        head_terms.astype(jnp.bfloat16), "mlp", scatter_dimension=1, tiled=True
    ).astype(jnp.float32)
    output_rank_rows = jnp.dot(
        attention_rows,
        output_down_maps.reshape(attention_rows.shape[1], ADAPTER_TOTAL * ADAPTER_RANK),
        preferred_element_type=jnp.float32,
    )
    output_rank_values = lax.psum(
        select_low(output_rank_rows, adapter_hot).astype(jnp.bfloat16), "mlp"
    )
    adapter_delta = jnp.dot(
        expand_rank_rows(output_rank_values, adapter_hot),
        output_up_maps.reshape(ADAPTER_TOTAL * ADAPTER_RANK, shard_hidden_width),
        preferred_element_type=jnp.float32,
    )
    blended_rows = (residual_rows.astype(jnp.float32) + projection_rows + adapter_delta).astype(
        jnp.bfloat16
    )
    values = blended_rows.astype(jnp.float32)
    full_rows = lax.all_gather(blended_rows, "mlp", axis=1, tiled=True).astype(jnp.float32)
    row_mean = jnp.sum(full_rows, axis=1, keepdims=True) / MODEL_WIDTH
    variance = (
        jnp.sum(full_rows * full_rows, axis=1, keepdims=True) / MODEL_WIDTH - row_mean * row_mean
    )
    normalized_rows = (
        (full_rows - row_mean) * lax.rsqrt(variance + norm_epsilon) * (1.0 + scale_rows)
        + shift_rows
    ).astype(jnp.bfloat16)
    normed_local = lax.dynamic_slice_in_dim(
        normalized_rows, column_index * shard_hidden_width, shard_hidden_width, 1
    )
    part_low = jnp.dot(
        normed_local,
        hidden_down_maps.reshape(shard_hidden_width, ADAPTER_TOTAL * ADAPTER_RANK),
        preferred_element_type=jnp.float32,
    )
    hidden_rank_values = lax.psum(select_low(part_low, adapter_hot).astype(jnp.bfloat16), "mlp")
    hidden_unit_width = up_weight.shape[1]
    hidden_total = jnp.dot(
        normalized_rows,
        lax.all_gather(up_weight, "req", axis=0, tiled=True),
        preferred_element_type=jnp.float32,
    )
    hidden_total = hidden_total + jnp.dot(
        expand_rank_rows(hidden_rank_values, adapter_hot),
        hidden_up_maps.reshape(ADAPTER_TOTAL * ADAPTER_RANK, hidden_unit_width),
        preferred_element_type=jnp.float32,
    )
    hidden = jax.nn.gelu(hidden_total, approximate=True).astype(jnp.bfloat16)
    down_terms = jnp.dot(
        hidden,
        lax.all_gather(down_weight, "req", axis=1, tiled=True),
        preferred_element_type=jnp.float32,
    )
    down_sum = lax.psum_scatter(
        down_terms.astype(jnp.bfloat16), "mlp", scatter_dimension=1, tiled=True
    ).astype(jnp.float32)
    return (values + gate_rows * down_sum).astype(jnp.bfloat16)


def local(
    residual_input,
    attention_output,
    request_length,
    request_group,
    adapter_per_group,
    output_weight,
    output_down_maps,
    output_up_maps,
    modulation,
    hidden_down_maps,
    hidden_up_maps,
    up_weight,
    down_weight,
):
    req_count = lax.axis_size("req")
    device_index = lax.axis_index("req")
    live_rows = jnp.sum(request_length, axis=1)
    dev_ends = jnp.cumsum(live_rows)
    dev_starts = dev_ends - live_rows
    offset = dev_starts[device_index]
    shard_hidden_width = residual_input.shape[1]
    weights = (
        request_length,
        request_group,
        adapter_per_group,
        output_weight,
        output_down_maps,
        output_up_maps,
        modulation,
        hidden_down_maps,
        hidden_up_maps,
        up_weight,
        down_weight,
    )
    token_rank = jnp.minimum(offset + jnp.arange(CAP, dtype=jnp.int32), TOK_DEV * req_count - 1)
    packed_out = layer_rows(attention_output, residual_input, token_rank, *weights)
    moved_out = lax.all_to_all(
        send_layout(packed_out, offset, req_count), "req", split_axis=1, concat_axis=1, tiled=True
    )
    result = compact(moved_out, dev_starts, dev_ends, req_count, device_index)
    return result.reshape(TOK_DEV, 1, shard_hidden_width)


def solution(mesh):
    placed = (
        P("req", "mlp"),
        P("req", "mlp"),
        P(),
        P(),
        P(),
        P("mlp", "req"),
        P("mlp", None, None),
        P(None, None, "mlp"),
        P(),
        P("mlp", None, None),
        P(None, None, "mlp"),
        P("req", "mlp"),
        P("mlp", "req"),
    )
    return jax.shard_map(
        local, mesh=mesh, in_specs=placed, out_specs=P(None, "req", "mlp"), check_vma=False
    )
```

profile of v0, /device:TPU:1, one launch (start us, length us, event | category | flops | bytes accessed | tf_op | source)
XLA Modules:
  0.0 416.4 jit_solution(15654548941162831555)
XLA Ops:
  6.5 0.7 all-gather.5.cloned.1.call-update
  7.3 55.5 %all-gather.5.cloned.1.call-done = bf16[384,5120]{0,1:T(8,128)(2,1)} async-done(((bf16[384,320]{0,1:T(8,128)(2,1)}), bf16[384,5120]{0,1:T(8,128)(2,1)}) %all-gather.5.cloned.1.call-update) | async-done | bytes 3932176 | tf_op jit(solution)/shard_map/all_gather | solution.py:91
  62.8 8.0 %convolution_convert_fusion.1 = bf16[576,5120]{1,0:T(8,128)(2,1)} fusion(bf16[576,384]{1,0:T(8,128)(2,1)} %param.14, bf16[384,5120]{0,1:T(8,128)(2,1)} %all-gather.5.cloned.1.call-done), kind=kOutput, calls=%fused_computation.13 | convolution fusion | flops 2267873280 | bytes 10272768 | tf_op jit(solution)/shard_map/dot_general | solution.py:89
  70.9 8.6 %copy.34 = bf16[576,5120]{0,1:T(8,128)(2,1)} copy(bf16[576,5120]{1,0:T(8,128)(2,1)} %convolution_convert_fusion.1) | data formatting | bytes 11796480
  79.7 0.6 copy-done.5
  80.8 0.6 dynamic_slice.15
  81.4 0.6 add_minimum_fusion
  82.8 23.1 %psum.14 = bf16[576,16]{0,1:T(8,128)(2,1)S(1)} all-reduce(bf16[576,16]{0,1:T(8,128)(2,1)S(1)} %fusion.18), channel_id=1, replica_groups=mesh['req'=16,'mlp'=8] {'mlp'}, use_global_device_ids=true, to_apply=%region_10.11 | all-reduce | flops 9216 | bytes 36864 | tf_op jit(solution)/shard_map/psum | solution.py:102
  105.9 17.0 %reduce-scatter.7.cloned.1.call-done = bf16[640,576]{1,0:T(8,128)(2,1)} async-done(((bf16[5120,576]{1,0:T(8,128)(2,1)}), bf16[640,576]{1,0:T(8,128)(2,1)}) %reduce-scatter.7.cloned.1.call-update) | async-done | bytes 737296
  122.9 1.5 copy.35
  124.5 1.3 fusion.16
  126.4 0.5 all-gather.11.cloned.1.call-update
  127.2 18.3 %fusion.22 = f32[576,3,5120]{2,0,1:T(8,128)} fusion(f32[8,3,5120]{2,0,1:T(8,128)S(1)} %copy-done, s32[576]{0:T(1024)S(1)} %select_reduce_fusion), kind=kOutput, calls=%fused_computation.38 | convolution fusion | flops 849351168 | bytes 35883264 | tf_op jit(solution)/shard_map/dot_general | solution.py:45
  145.5 20.5 %all-gather.7.cloned.1.call-done = bf16[576,5120]{1,0:T(8,128)(2,1)} async-done(((bf16[576,640]{1,0:T(8,128)(2,1)}), bf16[576,5120]{1,0:T(8,128)(2,1)}) %all-gather.7.cloned.1.call-update) | async-done | bytes 5898256 | tf_op jit(solution)/shard_map/all_gather | solution.py:114
  166.0 4.6 %convert_reduce_fusion = (f32[576]{0:T(1024)S(1)}, f32[576]{0:T(1024)S(1)}) fusion(bf16[576,5120]{1,0:T(8,128)(2,1)} %all-gather.7.cloned.1.call-done), kind=kLoop, calls=%fused_computation.3 | loop fusion | flops 11795328 | bytes 5902848 | tf_op jit(solution)/shard_map/reduce_sum | solution.py:115
  170.7 9.9 %fusion.3 = bf16[576,5120]{1,0:T(8,128)(2,1)S(1)} fusion(bf16[576,5120]{1,0:T(8,128)(2,1)S(1)} %copy-done.2, f32[576,3,5120]{2,0,1:T(8,128)} %fusion.22, f32[576]{0:T(1024)S(1)} %get-tuple-element.8, f32[576]{0:T(1024)S(1)} %get-tuple-element.7), kind=kLoop, calls=%fused_computation.7 | loop fusion | flops 20643840 | bytes 35394048 | tf_op jit(solution)/shard_map/convert_element_type | solution.py:122
  180.6 2.5 copy-done.3
  183.6 20.9 %psum.15 = bf16[576,16]{0,1:T(8,128)(2,1)S(1)} all-reduce(bf16[576,16]{0,1:T(8,128)(2,1)S(1)} %fusion.17), channel_id=1, replica_groups=mesh['req'=16,'mlp'=8] {'mlp'}, use_global_device_ids=true, to_apply=%region_14.15 | all-reduce | flops 9216 | bytes 36864 | tf_op jit(solution)/shard_map/psum | solution.py:131
  204.5 37.5 %all-gather.9.cloned.1.call-done = bf16[5120,864]{1,0:T(8,128)(2,1)} async-done(((bf16[320,864]{1,0:T(8,128)(2,1)}), bf16[5120,864]{1,0:T(8,128)(2,1)}) %all-gather.9.cloned.1.call-update) | async-done | bytes 8847376 | tf_op jit(solution)/shard_map/all_gather | solution.py:135
  242.0 11.9 %fusion.44 = f32[576,864]{1,0:T(8,128)} fusion(bf16[576,5120]{1,0:T(8,128)(2,1)} %copy-done.3, bf16[5120,864]{1,0:T(8,128)(2,1)} %all-gather.9.cloned.1.call-done), kind=kOutput, calls=%fused_computation.87 | convolution fusion | flops 5096079360 | bytes 16736256 | tf_op jit(solution)/shard_map/dot_general | solution.py:133
  253.9 64.2 %all-gather.11.cloned.1.call-done = bf16[864,5120]{0,1:T(8,128)(2,1)} async-done(((bf16[864,320]{0,1:T(8,128)(2,1)}), bf16[864,5120]{0,1:T(8,128)(2,1)}) %all-gather.11.cloned.1.call-update) | async-done | bytes 8847376 | tf_op jit(solution)/shard_map/all_gather | solution.py:146
  318.1 12.2 %convolution_convert_fusion = bf16[576,5120]{1,0:T(8,128)(2,1)} fusion(bf16[864,5120]{0,1:T(8,128)(2,1)} %all-gather.11.cloned.1.call-done, f32[576,864]{1,0:T(8,128)} %fusion.44, bf16[16,16,864]{2,1,0:T(8,128)(2,1)S(1)} %copy-done.9, bf16[576,16]{0,1:T(8,128)(2,1)S(1)} %psum.15, bf16[576,16]{0,1:T(8,128)(2,1)S(1)} %get-tuple-element.9), kind=kOutput, calls=%fused_computation.12 | convolution fusion | flops 5358956544 | bytes 17215488 | tf_op jit(solution)/shard_map/dot_general | solution.py:144
  330.3 8.6 %copy.36 = bf16[576,5120]{0,1:T(8,128)(2,1)} copy(bf16[576,5120]{1,0:T(8,128)(2,1)} %convolution_convert_fusion) | data formatting | bytes 11796480
  338.9 10.4 %slice.14 = f32[576,1,5120]{2,0,1:T(8,128)} slice(f32[576,3,5120]{2,0,1:T(8,128)} %fusion.22), slice={[0:576], [2:3], [0:5120]} | slice | bytes 23592960 | tf_op jit(solution)/shard_map/slice | solution.py:87
  351.2 30.8 %reduce-scatter.9.cloned.1.call-done = bf16[640,576]{1,0:T(8,128)(2,1)} async-done(((bf16[5120,576]{1,0:T(8,128)(2,1)}), bf16[640,576]{1,0:T(8,128)(2,1)}) %reduce-scatter.9.cloned.1.call-update) | async-done | bytes 737296
  382.0 1.5 copy.37
  383.5 1.6 fusion.15
  385.3 1.3 fusion.19
  386.5 6.7 %all-to-all-start = ((bf16[36,16,640]{2,0,1:T(8,128)(2,1)}), bf16[36,16,640]{2,0,1:T(8,128)(2,1)S(1)}, u32[]{:S(2)}, u32[]{:S(2)}) async-start(bf16[36,16,640]{2,0,1:T(8,128)(2,1)} %fusion.19), calls=%async_computation | async-start | bytes 1638400 | tf_op jit(solution)/shard_map/all_to_all | solution.py:192
  393.5 12.9 %all-to-all-done = bf16[36,16,640]{2,0,1:T(8,128)(2,1)S(1)} async-done(((bf16[36,16,640]{2,0,1:T(8,128)(2,1)}), bf16[36,16,640]{2,0,1:T(8,128)(2,1)S(1)}, u32[]{:S(2)}, u32[]{:S(2)}) %all-to-all-start) | async-done | bytes 737312 | tf_op jit(solution)/shard_map/all_to_all | solution.py:192
  406.4 2.2 gather_fusion
  408.6 0.9 bitcast_select_fusion
  (61 shorter events, 3.3 us)
Async XLA Ops:
  6.5 120.7 %copy-start = (f32[8,3,5120]{2,0,1:T(8,128)S(1)}, f32[8,3,5120]{2,0,1:T(8,128)}, u32[]{:S(2)}) copy-start(f32[8,3,5120]{2,0,1:T(8,128)} %param.21) | copy-start | bytes 1474564
  6.5 56.3 %all-gather.5.cloned.1.call-start = ((), (), s32[]{:S(2)}) async-start(), calls=%async_computation.3 | async-start | bytes 4177920 | tf_op jit(solution)/shard_map/all_gather | solution.py:91
  7.3 115.7 %reduce-scatter.7.cloned.1.call-start = ((), (), s32[]{:S(2)}) async-start(), calls=%async_computation.7 | async-start | bytes 7372800
  79.5 0.7 copy-start.5
  79.5 2.7 copy-start.6
  79.5 2.8 copy-start.7
  79.5 2.9 copy-start.10
  79.5 2.9 copy-start.13
  79.5 44.9 %copy-start.8 = (bf16[576,640]{1,0:T(8,128)(2,1)S(1)}, bf16[576,640]{1,0:T(8,128)(2,1)}, u32[]{:S(2)}) copy-start(bf16[576,640]{1,0:T(8,128)(2,1)} %param.13) | copy-start | bytes 2211844
  79.6 44.9 %copy-start.11 = (bf16[16,16,640]{2,1,0:T(8,128)(2,1)S(1)}, bf16[16,16,640]{2,1,0:T(8,128)(2,1)}, u32[]{:S(2)}) copy-start(bf16[16,16,640]{2,1,0:T(8,128)(2,1)} %param.20) | copy-start | bytes 983044
  79.6 86.4 %all-gather.7.cloned.1.call-start = ((), (), s32[]{:S(2)}) async-start(), calls=%async_computation.4 | async-start | bytes 6635520 | tf_op jit(solution)/shard_map/all_gather | solution.py:114
  125.8 116.2 %all-gather.9.cloned.1.call-start = ((), (), s32[]{:S(2)}) async-start(), calls=%async_computation.5 | async-start | bytes 9748480 | tf_op jit(solution)/shard_map/all_gather | solution.py:135
  126.4 191.7 %all-gather.11.cloned.1.call-start = ((), (), s32[]{:S(2)}) async-start(), calls=%async_computation.6 | async-start | bytes 9748480 | tf_op jit(solution)/shard_map/all_gather | solution.py:146
  127.0 255.0 %reduce-scatter.9.cloned.1.call-start = ((), (), s32[]{:S(2)}) async-start(), calls=%async_computation.8 | async-start | bytes 7372800
  166.0 4.6 %copy-start.2 = (bf16[576,5120]{1,0:T(8,128)(2,1)S(1)}, bf16[576,5120]{1,0:T(8,128)(2,1)}, u32[]{:S(2)}) copy-start(bf16[576,5120]{1,0:T(8,128)(2,1)} %all-gather.7.cloned.1.call-done) | copy-start | bytes 17694724
  170.7 12.4 %copy-start.12 = (bf16[640,16,16]{0,2,1:T(8,128)(2,1)S(1)}, bf16[640,16,16]{0,2,1:T(8,128)(2,1)}, u32[]{:S(2)}) copy-start(bf16[640,16,16]{0,2,1:T(8,128)(2,1)} %param.22) | copy-start | bytes 983044
  180.6 2.5 copy-start.3
  204.5 113.6 %copy-start.9 = (bf16[16,16,864]{2,1,0:T(8,128)(2,1)S(1)}, bf16[16,16,864]{2,1,0:T(8,128)(2,1)}, u32[]{:S(2)}) copy-start(bf16[16,16,864]{2,1,0:T(8,128)(2,1)} %param.23) | copy-start | bytes 1327108
  338.9 44.6 %copy-start.4 = (bf16[576,640]{1,0:T(8,128)(2,1)S(1)}, bf16[576,640]{1,0:T(8,128)(2,1)}, u32[]{:S(2)}) copy-start(bf16[576,640]{1,0:T(8,128)(2,1)} %fusion.16) | copy-start | bytes 2211844
  385.1 24.5 %copy-start.1 = (f32[8,3,5120]{2,0,1:T(8,128)S(1)}, f32[8,3,5120]{2,0,1:T(8,128)}, u32[]{:S(2)}) copy-start(f32[8,3,5120]{2,0,1:T(8,128)} %param.21) | copy-start | bytes 1474564
  386.5 19.8 %all-to-all-start = ((bf16[36,16,640]{2,0,1:T(8,128)(2,1)}), bf16[36,16,640]{2,0,1:T(8,128)(2,1)S(1)}, u32[]{:S(2)}, u32[]{:S(2)}) async-start(bf16[36,16,640]{2,0,1:T(8,128)(2,1)} %fusion.19), calls=%async_computation | async-start | bytes 1638400 | tf_op jit(solution)/shard_map/all_to_all | solution.py:192
Sparse Core Ops, SparseCore 0:
  9.5 53.3 all-gather.4
  79.7 43.1 reduce-scatter.6
  125.9 40.0 all-gather.6
  168.0 73.9 all-gather.8
  244.0 74.0 all-gather.10
  339.0 42.9 reduce-scatter.8
where the time goes:
time: 420 us; the launch traced here: 416 us
  waiting for transfers between devices  240 us (57%)
  matrix products  52.6 us (13%)
  blocking collectives  44 us (10%)
  local copies, waits for them, and re-layouts  37 us (9%)
  other arithmetic  19.9 us (5%)
  between operations  15.7 us (4%)
  starting transfers between devices  7.04 us (2%)
    all_gather x1, waiting for transfers between devices, layer_rows(): lax.all_gather(down_weight, 'req', axis=1, tiled=True)  64.2 us
    all_gather x1, waiting for transfers between devices, layer_rows(): lax.all_gather(output_weight, 'req', axis=1, tiled=True)  55.5 us
    unnamed x8, waiting for transfers between devices  49.6 us
    all_gather x1, waiting for transfers between devices, layer_rows(): lax.all_gather(up_weight, 'req', axis=0, tiled=True)  37.5 us
    unnamed x33, local copies, waits for them, and re-layouts  23.4 us
    psum x1, blocking collectives, layer_rows(): lax.psum(select_low(output_rank_rows, adapter_hot).astype(jnp.bfloat16),...  23.1 us
    psum x1, blocking collectives, layer_rows(): lax.psum(select_low(part_low, adapter_hot).astype(jnp.bfloat16), 'mlp')  20.9 us
    all_gather x1, waiting for transfers between devices, layer_rows(): lax.all_gather(blended_rows, 'mlp', axis=1, tiled=True).astype(jnp.float32)  20.5 us
  transfers between devices with their start and end apart: 7, of which 7 were waited for; matrix products, arithmetic and copies ran while one was open for 14% of the time, Pallas kernels for 0%

commit v1 on v0

v1 whole, which is shorter than its diff:
```python
import jax
import jax.numpy as jnp
from jax import lax
from jax.sharding import PartitionSpec as P

MODEL_WIDTH = 5120
ADAPTER_RANK = 16
ADAPTER_TOTAL = 16
TOK_DEV = 384


norm_epsilon = 1e-06


def send_layout(packed, offset, req_count):
    shaped = packed.reshape(packed.shape[0] // req_count, req_count, packed.shape[1])
    return jnp.roll(shaped, offset, axis=1)


def compact(moved, starts, ends, req_count, token_rank):
    slots = moved.shape[0] * moved.shape[1]
    flat_rows = moved.reshape(slots, moved.shape[2])
    source = jnp.sum((ends[None, :] <= token_rank[:, None]).astype(jnp.int32), axis=1)
    source_hot = source[:, None] == jnp.arange(req_count, dtype=jnp.int32)[None, :]
    source_start = jnp.sum(jnp.where(source_hot, starts[None, :], 0), axis=1)
    position = (token_rank - source_start) // req_count * req_count + source
    return jnp.take(flat_rows, position, axis=0)


def token_groups(token_rank, request_length, request_group, adapter_per_group):
    req_ends = jnp.cumsum(request_length.reshape(-1))
    request_count = req_ends.shape[0]
    request = jnp.sum((req_ends[None, :] <= token_rank[:, None]).astype(jnp.int32), axis=1)
    request = jnp.minimum(request, request_count - 1)
    request_hot = request[:, None] == jnp.arange(request_count, dtype=jnp.int32)[None, :]
    group_ids = jnp.sum(jnp.where(request_hot, request_group[None, :], 0), axis=1)
    group_count = adapter_per_group.shape[0]
    group_hot = group_ids[:, None] == jnp.arange(group_count, dtype=jnp.int32)[None, :]
    adapter_of_row = jnp.sum(jnp.where(group_hot, adapter_per_group[None, :], 0), axis=1)
    adapter_hot = (
        adapter_of_row[:, None] == jnp.arange(ADAPTER_TOTAL, dtype=jnp.int32)[None, :]
    ).astype(jnp.float32)
    return group_ids, adapter_hot


def select_low(output_rank_rows, adapter_hot):
    shaped = output_rank_rows.reshape(output_rank_rows.shape[0], ADAPTER_TOTAL, ADAPTER_RANK)
    return jnp.sum(shaped * adapter_hot[:, :, None], axis=1)


def expand_rank_rows(low_rows, adapter_hot):
    spread_rows = adapter_hot.astype(jnp.bfloat16)[:, :, None] * low_rows[:, None, :]
    return spread_rows.reshape(low_rows.shape[0], ADAPTER_TOTAL * ADAPTER_RANK)


def mlp_sum(part):
    n = lax.axis_size("mlp")
    total = part.astype(jnp.float32)
    for k in range(1, n):
        moved = lax.ppermute(part, "mlp", [(i, (i + k) % n) for i in range(n)])
        total = total + moved.astype(jnp.float32)
    return total


def local(
    residual_input,
    attention_output,
    request_length,
    request_group,
    adapter_per_group,
    output_weight,
    output_down_maps,
    output_up_maps,
    modulation,
    hidden_down_maps,
    hidden_up_maps,
    up_weight,
    down_weight,
):
    req_count = lax.axis_size("req")
    mlp_count = lax.axis_size("mlp")
    device_index = lax.axis_index("req")
    column_index = lax.axis_index("mlp")
    width = residual_input.shape[1]
    head_width = attention_output.shape[1]

    out_w = lax.all_gather(output_weight, "req", axis=1, tiled=True)
    up_w = lax.all_gather(up_weight, "req", axis=0, tiled=True)
    down_w = lax.all_gather(down_weight, "req", axis=1, tiled=True)

    live_rows = jnp.sum(request_length, axis=1)
    dev_ends = jnp.cumsum(live_rows)
    dev_starts = dev_ends - live_rows
    offset = dev_starts[device_index]
    tok_dev = TOK_DEV
    token_rank = jnp.arange(tok_dev, dtype=jnp.int32) * req_count + device_index
    moved_attn = lax.all_to_all(
        send_layout(attention_output, offset, req_count), "req", split_axis=1, concat_axis=1, tiled=True
    )
    attention_rows = compact(moved_attn, dev_starts, dev_ends, req_count, token_rank)
    moved_res = lax.all_to_all(
        send_layout(residual_input, offset, req_count), "req", split_axis=1, concat_axis=1, tiled=True
    )
    residual_rows = compact(moved_res, dev_starts, dev_ends, req_count, token_rank)

    group_ids, adapter_hot = token_groups(token_rank, request_length, request_group, adapter_per_group)
    shift_rows = jnp.take(modulation[:, 0, :], group_ids, axis=0)
    scale_rows = jnp.take(modulation[:, 1, :], group_ids, axis=0)
    gate_table = lax.dynamic_slice_in_dim(modulation[:, 2, :], column_index * width, width, 1)
    gate_rows = jnp.take(gate_table, group_ids, axis=0)

    head_terms = jnp.einsum(
        "tk,kmc->mtc",
        attention_rows,
        out_w.reshape(head_width, mlp_count, width),
        preferred_element_type=jnp.float32,
    )
    out_low = select_low(
        jnp.dot(
            attention_rows,
            output_down_maps.reshape(head_width, ADAPTER_TOTAL * ADAPTER_RANK),
            preferred_element_type=jnp.float32,
        ),
        adapter_hot,
    )
    send = jnp.concatenate(
        [head_terms, jnp.broadcast_to(out_low[None], (mlp_count,) + out_low.shape)], axis=2
    ).astype(jnp.bfloat16)
    summed = lax.psum_scatter(send, "mlp", scatter_dimension=0, tiled=True)[0]
    projection_rows = summed[:, :width].astype(jnp.float32)
    output_rank_values = summed[:, width:]
    adapter_delta = jnp.dot(
        expand_rank_rows(output_rank_values, adapter_hot),
        output_up_maps.reshape(ADAPTER_TOTAL * ADAPTER_RANK, width),
        preferred_element_type=jnp.float32,
    )
    blended_rows = (residual_rows.astype(jnp.float32) + projection_rows + adapter_delta).astype(
        jnp.bfloat16
    )
    values = blended_rows.astype(jnp.float32)

    full_rows = lax.all_gather(blended_rows, "mlp", axis=0, tiled=False).astype(jnp.float32)
    row_mean = jnp.sum(full_rows, axis=(0, 2)) / MODEL_WIDTH
    variance = jnp.sum(full_rows * full_rows, axis=(0, 2)) / MODEL_WIDTH - row_mean * row_mean
    inv = lax.rsqrt(variance + norm_epsilon)
    scale_m = (1.0 + scale_rows).reshape(-1, mlp_count, width).transpose(1, 0, 2)
    shift_m = shift_rows.reshape(-1, mlp_count, width).transpose(1, 0, 2)
    normalized = (
        (full_rows - row_mean[None, :, None]) * inv[None, :, None] * scale_m + shift_m
    ).astype(jnp.bfloat16)

    normed_local = lax.dynamic_index_in_dim(normalized, column_index, 0, keepdims=False)
    part_low = jnp.dot(
        normed_local,
        hidden_down_maps.reshape(width, ADAPTER_TOTAL * ADAPTER_RANK),
        preferred_element_type=jnp.float32,
    )
    hidden_rank_values = mlp_sum(select_low(part_low, adapter_hot).astype(jnp.bfloat16)).astype(
        jnp.bfloat16
    )
    hidden_units = up_weight.shape[1]
    hidden_total = jnp.einsum(
        "mtc,mch->th",
        normalized,
        up_w.reshape(mlp_count, width, hidden_units),
        preferred_element_type=jnp.float32,
    )
    hidden_total = hidden_total + jnp.dot(
        expand_rank_rows(hidden_rank_values, adapter_hot),
        hidden_up_maps.reshape(ADAPTER_TOTAL * ADAPTER_RANK, hidden_units),
        preferred_element_type=jnp.float32,
    )
    hidden = jax.nn.gelu(hidden_total, approximate=True).astype(jnp.bfloat16)
    down_terms = jnp.einsum(
        "th,hmc->mtc",
        hidden,
        down_w.reshape(hidden_units, mlp_count, width),
        preferred_element_type=jnp.float32,
    ).astype(jnp.bfloat16)
    down_sum = lax.psum_scatter(down_terms, "mlp", scatter_dimension=0, tiled=True)[0].astype(
        jnp.float32
    )
    result = (values + gate_rows * down_sum).astype(jnp.bfloat16)
    return result.reshape(tok_dev, 1, width)


def solution(mesh):
    placed = (
        P("req", "mlp"),
        P("req", "mlp"),
        P(),
        P(),
        P(),
        P("mlp", "req"),
        P("mlp", None, None),
        P(None, None, "mlp"),
        P(),
        P("mlp", None, None),
        P(None, None, "mlp"),
        P("req", "mlp"),
        P("mlp", "req"),
    )
    return jax.shard_map(
        local, mesh=mesh, in_specs=placed, out_specs=P(None, "req", "mlp"), check_vma=False
    )
```

time: 420 us -> 354 us (0.84)
  matrix products: 52.6 us -> 26.1 us
  blocking collectives: 44 us -> 18.5 us
  waiting for transfers between devices: 240 us -> 218 us
  local copies, waits for them, and re-layouts: 37 us -> 24 us
  other arithmetic: 19.9 us -> 32.5 us
  starting transfers between devices: 7.04 us -> 16.5 us
    unnamed x8 -> x6, waiting for transfers between devices: 49.6 us -> 1.82 us
    reduce_scatter x0 -> x2, waiting for transfers between devices: none -> 46.2 us  [the longest x1 32.5 us: local(): lax.psum_scatter(down_terms, 'mlp', scatter_dimension=0, tiled=True)[0]]
    psum x2 -> x0, blocking collectives: 44 us -> none  [the longest x1 23.1 us: layer_rows(): lax.psum(select_low(output_rank_rows, adapter_hot).astype(jnp.bfloat16),...]
    dot_general x7 -> x6, matrix products: 52.6 us -> 26.1 us  [the longest x1 9.56 us: local(): jnp.einsum('mtc,mch->th', normalized, up_w.reshape(mlp_count, width, hidd...]
    unnamed x33 -> x17, local copies, waits for them, and re-layouts: 23.4 us -> 3.75 us
    all_to_all x0 -> x1, blocking collectives: none -> 18.5 us  [local(): lax.all_to_all(send_layout(residual_input, offset, req_count), 'req', spl...]
    all_gather x4, waiting for transfers between devices: 178 us -> 161 us  [the longest x1 66.4 us: local(): down_w = lax.all_gather(down_weight, 'req', axis=1, tiled=True)]
    gather x0 -> x3, local copies, waits for them, and re-layouts: none -> 12.7 us  [the longest x1 5.49 us: local(): shift_rows = jnp.take(modulation[:, 0, :], group_ids, axis=0)]
  transfers between devices with their start and end apart: 7 -> 14, of which waited for: 7 -> 7; matrix products, arithmetic and copies ran while one was open for 14% -> 17% of each run, Pallas kernels for 0% -> 0%
where the time goes in v1:
time: 354 us; the launch traced here: 351 us
  waiting for transfers between devices  218 us (62%)
  other arithmetic  32.5 us (9%)
  matrix products  26.1 us (7%)
  local copies, waits for them, and re-layouts  24 us (7%)
  blocking collectives  18.5 us (5%)
  starting transfers between devices  16.5 us (5%)
  between operations  15.8 us (4%)
    all_gather x1, waiting for transfers between devices, local(): down_w = lax.all_gather(down_weight, 'req', axis=1, tiled=True)  66.4 us
    all_gather x1, waiting for transfers between devices, local(): up_w = lax.all_gather(up_weight, 'req', axis=0, tiled=True)  53.5 us
    reduce_scatter x1, waiting for transfers between devices, local(): lax.psum_scatter(down_terms, 'mlp', scatter_dimension=0, tiled=True)[0]  32.5 us
    all_gather x1, waiting for transfers between devices, local(): out_w = lax.all_gather(output_weight, 'req', axis=1, tiled=True)  30.7 us
    all_to_all x1, blocking collectives, local(): lax.all_to_all(send_layout(residual_input, offset, req_count), 'req', spl...  18.5 us
    reduce_scatter x1, waiting for transfers between devices, local(): summed = lax.psum_scatter(send, 'mlp', scatter_dimension=0, tiled=True)[0]  13.7 us
    add x1, other arithmetic, local(): 1.0 + scale_rows  10.5 us
    all_gather x1, waiting for transfers between devices, local(): lax.all_gather(blended_rows, 'mlp', axis=0, tiled=False).astype(jnp.float32)  10.5 us
  transfers between devices with their start and end apart: 14, of which 7 were waited for; matrix products, arithmetic and copies ran while one was open for 17% of the time, Pallas kernels for 0%

profile of v1, /device:TPU:1, one launch (start us, length us, event | category | flops | bytes accessed | tf_op | source)
XLA Modules:
  0.0 351.3 jit_solution(11191218446794907025)
XLA Ops:
  10.8 1.4 fusion.27
  13.0 8.4 %all-to-all-start.1 = ((bf16[36,16,384]{2,0,1:T(8,128)(2,1)}), bf16[36,16,384]{2,0,1:T(8,128)(2,1)S(1)}, u32[]{:S(2)}, u32[]{:S(2)}) async-start(bf16[36,16,384]{2,0,1:T(8,128)(2,1)} %copy.64), calls=%async_computation.1 | async-start | bytes 983040 | tf_op jit(solution)/shard_map/all_to_all | solution.py:97
  24.4 8.8 %all-to-all-done.1 = bf16[36,16,384]{2,0,1:T(8,128)(2,1)S(1)} async-done(((bf16[36,16,384]{2,0,1:T(8,128)(2,1)}), bf16[36,16,384]{2,0,1:T(8,128)(2,1)S(1)}, u32[]{:S(2)}, u32[]{:S(2)}) %all-to-all-start.1) | async-done | bytes 442400 | tf_op jit(solution)/shard_map/all_to_all | solution.py:97
  33.2 2.1 gather_fusion.1
  35.9 30.7 %all-gather.6.cloned.1.call-done = bf16[384,5120]{0,1:T(8,128)(2,1)} async-done(((bf16[384,320]{0,1:T(8,128)(2,1)}), bf16[384,5120]{0,1:T(8,128)(2,1)}) %all-gather.6.cloned.1.call-update) | async-done | bytes 3932176 | tf_op jit(solution)/shard_map/all_gather | solution.py:87
  66.6 4.4 %convert_bitcast_fusion.1 = bf16[8,384,640]{2,1,0:T(8,128)(2,1)S(1)} fusion(bf16[384,8,640]{0,2,1:T(8,128)(2,1)} %bitcast.111, bf16[384,384]{1,0:T(8,128)(2,1)S(1)} %gather_fusion.1, pred[384]{0:T(512)(128)(4,1)S(1)} %compare_and_fusion.1), kind=kOutput, calls=%fused_computation.15 | convolution fusion | flops 1512062976 | bytes 8159616 | tf_op jit(solution)/shard_map/tk,kmc->mtc/dot_general | solution.py:112
  71.1 2.7 pad_maximum_fusion
  73.8 1.0 copy-done.3
  75.6 18.5 %all_to_all.10 = bf16[36,16,640]{2,0,1:T(8,128)(2,1)S(1)} all-to-all(bf16[36,16,640]{2,0,1:T(8,128)(2,1)S(1)} %copy.62), channel_id=1, replica_groups=mesh['req'=16,'mlp'=8] {'req'}, dimensions={1} | all-to-all | bytes 1474560 | tf_op jit(solution)/shard_map/all_to_all | solution.py:101
  94.2 2.2 gather_fusion
  96.4 13.7 %reduce-scatter.3.cloned.1.call-done = bf16[1,384,656]{2,1,0:T(8,128)(2,1)} async-done(((bf16[8,384,656]{2,1,0:T(8,128)(2,1)}), bf16[1,384,656]{2,1,0:T(8,128)(2,1)}) %reduce-scatter.3.cloned.1.call-update) | async-done | bytes 503824 | tf_op jit(solution)/shard_map/reduce_scatter | solution.py:129
  111.1 2.2 fusion.13
  114.9 5.4 %gather_fusion.3 = f32[384,5120]{1,0:T(8,128)} fusion(f32[8,5120]{1,0:T(8,128)S(1)} %get-tuple-element.8, s32[1024]{0:T(1024)S(1)} %pad_clamp_fusion), kind=kCustom, calls=%fused_computation.clone | custom fusion | bytes 15730176 | tf_op jit(solution)/shard_map/jit(_take)/gather | solution.py:108
  120.2 5.5 %gather_fusion.4 = f32[384,5120]{1,0:T(8,128)} fusion(f32[8,5120]{1,0:T(8,128)S(1)} %get-tuple-element.10, s32[1024]{0:T(1024)S(1)} %pad_clamp_fusion), kind=kCustom, calls=%fused_computation.1.clone | custom fusion | bytes 15730176 | tf_op jit(solution)/shard_map/jit(_take)/gather | solution.py:107
  125.7 10.5 %select_add_fusion = (f32[384,5120]{1,0:T(8,128)}, f32[384,5120]{1,0:T(8,128)}) fusion(f32[384,5120]{1,0:T(8,128)} %gather_fusion.3, pred[384]{0:T(512)(128)(4,1)S(1)} %compare_and_fusion, f32[384,5120]{1,0:T(8,128)} %gather_fusion.4), kind=kLoop, calls=%fused_computation.10 | loop fusion | flops 5898240 | bytes 31457664 | tf_op jit(solution)/shard_map/add | solution.py:146
  136.3 10.5 %all-gather.12.cloned.1.call-done = bf16[3072,640]{1,0:T(8,128)(2,1)} async-done(((bf16[384,640]{1,0:T(8,128)(2,1)}), bf16[3072,640]{1,0:T(8,128)(2,1)}) %all-gather.12.cloned.1.call-update) | async-done | bytes 3932176 | tf_op jit(solution)/shard_map/all_gather | solution.py:142
  146.8 2.7 convert_reduce_fusion
  149.5 3.0 multiply_reduce_fusion
  152.5 6.6 %fusion.1 = bf16[8,384,640]{2,1,0:T(8,128)(2,1)S(1)} fusion(f32[48,8,8,640]{3,2,1,0:T(8,128)} %bitcast.107, f32[48,8,8,640]{3,2,1,0:T(8,128)} %bitcast.106, f32[8,384,640]{2,1,0:T(8,128)S(1)} %get-tuple-element.7, f32[384]{0:T(512)S(1)} %get-tuple-element.12, f32[384]{0:T(512)S(1)} %get-tuple-element.11), kind=kLoop, calls=%fused_computation.7 | loop fusion | flops 9830400 | bytes 27528192 | tf_op jit(solution)/shard_map/convert_element_type | solution.py:150
  159.2 1.9 copy-done.1
  161.7 0.9 collective-permute-start.1
  162.6 1.2 collective-permute-start.2
  163.8 1.7 collective-permute-start.3
  165.4 2.6 collective-permute-start.4
  168.1 1.1 collective-permute-start.6
  169.1 53.5 %all-gather.8.cloned.1.call-done = bf16[5120,864]{1,0:T(8,128)(2,1)} async-done(((bf16[320,864]{1,0:T(8,128)(2,1)}), bf16[5120,864]{1,0:T(8,128)(2,1)}) %all-gather.8.cloned.1.call-update) | async-done | bytes 8847376 | tf_op jit(solution)/shard_map/all_gather | solution.py:88
  222.7 9.6 %convolution_bitcast_fusion.1 = f32[384,864]{0,1:T(8,128)S(1)} fusion(bf16[8,384,640]{2,1,0:T(8,128)(2,1)} %copy-done.1, bf16[8,640,864]{2,1,0:T(8,128)(2,1)} %bitcast.118), kind=kOutput, calls=%fused_computation.21 | convolution fusion | flops 3397386240 | bytes 14106624 | tf_op jit(solution)/shard_map/mtc,mch->th/dot_general | solution.py:162
  232.3 66.4 %all-gather.10.cloned.1.call-done = bf16[864,5120]{0,1:T(8,128)(2,1)} async-done(((bf16[864,320]{0,1:T(8,128)(2,1)}), bf16[864,5120]{0,1:T(8,128)(2,1)}) %all-gather.10.cloned.1.call-update) | async-done | bytes 8847376 | tf_op jit(solution)/shard_map/all_gather | solution.py:89
  298.8 9.1 %convert_bitcast_fusion = bf16[8,384,640]{2,1,0:T(8,128)(2,1)} fusion(bf16[864,8,640]{0,2,1:T(8,128)(2,1)} %bitcast.117, f32[384,864]{0,1:T(8,128)S(1)} %convolution_bitcast_fusion.1, bf16[16,16,864]{2,1,0:T(8,128)(2,1)S(1)} %copy-done, bf16[384,16]{0,1:T(8,128)(2,1)S(1)} %add_convert_fusion, bf16[384,16]{0,1:T(8,128)(2,1)S(1)} %get-tuple-element.13), kind=kOutput, calls=%fused_computation.14 | convolution fusion | flops 3572637696 | bytes 14573568 | tf_op jit(solution)/shard_map/th,hmc->mtc/dot_general | solution.py:174
  308.0 1.9 gather_fusion.2
  309.9 32.5 %reduce-scatter.5.cloned.1.call-done = bf16[1,384,640]{2,1,0:T(8,128)(2,1)} async-done(((bf16[8,384,640]{2,1,0:T(8,128)(2,1)}), bf16[1,384,640]{2,1,0:T(8,128)(2,1)}) %reduce-scatter.5.cloned.1.call-update) | async-done | bytes 491536 | tf_op jit(solution)/shard_map/reduce_scatter | solution.py:180
  342.3 2.1 fusion.24
  (78 shorter events, 10.7 us)
Async XLA Ops:
  6.5 292.2 %copy-start = (bf16[16,16,864]{2,1,0:T(8,128)(2,1)S(1)}, bf16[16,16,864]{2,1,0:T(8,128)(2,1)}, u32[]{:S(2)}) copy-start(bf16[16,16,864]{2,1,0:T(8,128)(2,1)} %param.25) | copy-start | bytes 1327108
  6.5 28.8 %copy-start.7 = (bf16[384,16,16]{0,2,1:T(8,128)(2,1)S(1)}, bf16[384,16,16]{0,2,1:T(8,128)(2,1)}, u32[]{:S(2)}) copy-start(bf16[384,16,16]{0,2,1:T(8,128)(2,1)} %param.21) | copy-start | bytes 589828
  6.5 60.0 %all-gather.6.cloned.1.call-start = ((), (), s32[]{:S(2)}) async-start(), calls=%async_computation.4 | async-start | bytes 4177920 | tf_op jit(solution)/shard_map/all_gather | solution.py:87
  13.0 20.1 %all-to-all-start.1 = ((bf16[36,16,384]{2,0,1:T(8,128)(2,1)}), bf16[36,16,384]{2,0,1:T(8,128)(2,1)S(1)}, u32[]{:S(2)}, u32[]{:S(2)}) async-start(bf16[36,16,384]{2,0,1:T(8,128)(2,1)} %copy.64), calls=%async_computation.1 | async-start | bytes 983040 | tf_op jit(solution)/shard_map/all_to_all | solution.py:97
  21.4 88.7 %reduce-scatter.3.cloned.1.call-start = ((), (), s32[]{:S(2)}) async-start(), calls=%async_computation.5 | async-start | bytes 5308416 | tf_op jit(solution)/shard_map/reduce_scatter | solution.py:129
  73.7 1.1 copy-start.3
  73.7 73.0 %all-gather.12.cloned.1.call-start = ((), (), s32[]{:S(2)}) async-start(), calls=%async_computation.9 | async-start | bytes 4423680 | tf_op jit(solution)/shard_map/all_gather | solution.py:142
  75.4 35.7 %copy-start.5 = (bf16[16,16,640]{2,1,0:T(8,128)(2,1)S(1)}, bf16[16,16,640]{2,1,0:T(8,128)(2,1)}, u32[]{:S(2)}) copy-start(bf16[16,16,640]{2,1,0:T(8,128)(2,1)} %param.22) | copy-start | bytes 983044
  111.1 3.7 %copy-start.4 = (f32[8,3,5120]{2,0,1:T(8,128)S(1)}, f32[8,3,5120]{2,0,1:T(8,128)}, u32[]{:S(2)}) copy-start(f32[8,3,5120]{2,0,1:T(8,128)} %param.23) | copy-start | bytes 1474564
  113.4 109.3 %all-gather.8.cloned.1.call-start = ((), (), s32[]{:S(2)}) async-start(), calls=%async_computation.6 | async-start | bytes 9748480 | tf_op jit(solution)/shard_map/all_gather | solution.py:88
  114.0 184.8 %all-gather.10.cloned.1.call-start = ((), (), s32[]{:S(2)}) async-start(), calls=%async_computation.7 | async-start | bytes 9748480 | tf_op jit(solution)/shard_map/all_gather | solution.py:89
  114.6 227.8 %reduce-scatter.5.cloned.1.call-start = ((), (), s32[]{:S(2)}) async-start(), calls=%async_computation.8 | async-start | bytes 4423680 | tf_op jit(solution)/shard_map/reduce_scatter | solution.py:180
  152.5 8.5 %copy-start.6 = (bf16[640,16,16]{0,2,1:T(8,128)(2,1)S(1)}, bf16[640,16,16]{0,2,1:T(8,128)(2,1)}, u32[]{:S(2)}) copy-start(bf16[640,16,16]{0,2,1:T(8,128)(2,1)} %param.24) | copy-start | bytes 983044
  159.2 1.9 copy-start.1
  161.4 6.6 %collective-permute-start = (bf16[384,16]{0,1:T(8,128)(2,1)S(1)}, bf16[384,16]{0,1:T(8,128)(2,1)S(1)}, u32[]{:S(2)}, u32[]{:S(2)}) collective-permute-start(bf16[384,16]{0,1:T(8,128)(2,1)S(1)} %fusion.16), channel_id=1, source_target_pairs={{0,1},{1,2},{2,3},{3,4},{4,5},{5,6},{6,7},{7,0},{8,9},{9,10},{10,1... | collective-permute-start | bytes 36872 | tf_op jit(solution)/shard_map/ppermute | solution.py:60
  161.7 6.4 %collective-permute-start.1 = (bf16[384,16]{0,1:T(8,128)(2,1)S(1)}, bf16[384,16]{0,1:T(8,128)(2,1)S(1)}, u32[]{:S(2)}, u32[]{:S(2)}) collective-permute-start(bf16[384,16]{0,1:T(8,128)(2,1)S(1)} %fusion.16), channel_id=1, source_target_pairs={{0,2},{1,3},{2,4},{3,5},{4,6},{5,7},{6,0},{7,1},{8,10},{9,11},{10,... | collective-permute-start | bytes 36872 | tf_op jit(solution)/shard_map/ppermute | solution.py:60
  162.6 69.6 %collective-permute-start.2 = (bf16[384,16]{0,1:T(8,128)(2,1)S(1)}, bf16[384,16]{0,1:T(8,128)(2,1)S(1)}, u32[]{:S(2)}, u32[]{:S(2)}) collective-permute-start(bf16[384,16]{0,1:T(8,128)(2,1)S(1)} %fusion.16), channel_id=1, source_target_pairs={{0,3},{1,4},{2,5},{3,6},{4,7},{5,0},{6,1},{7,2},{8,11},{9,12},{10,... | collective-permute-start | bytes 36872 | tf_op jit(solution)/shard_map/ppermute | solution.py:60
  163.8 68.5 %collective-permute-start.3 = (bf16[384,16]{0,1:T(8,128)(2,1)S(1)}, bf16[384,16]{0,1:T(8,128)(2,1)S(1)}, u32[]{:S(2)}, u32[]{:S(2)}) collective-permute-start(bf16[384,16]{0,1:T(8,128)(2,1)S(1)} %fusion.16), channel_id=1, source_target_pairs={{0,4},{1,5},{2,6},{3,7},{4,0},{5,1},{6,2},{7,3},{8,12},{9,13},{10,... | collective-permute-start | bytes 36872 | tf_op jit(solution)/shard_map/ppermute | solution.py:60
  165.4 66.8 %collective-permute-start.4 = (bf16[384,16]{0,1:T(8,128)(2,1)S(1)}, bf16[384,16]{0,1:T(8,128)(2,1)S(1)}, u32[]{:S(2)}, u32[]{:S(2)}) collective-permute-start(bf16[384,16]{0,1:T(8,128)(2,1)S(1)} %fusion.16), channel_id=1, source_target_pairs={{0,5},{1,6},{2,7},{3,0},{4,1},{5,2},{6,3},{7,4},{8,13},{9,14},{10,... | collective-permute-start | bytes 36872 | tf_op jit(solution)/shard_map/ppermute | solution.py:60
  168.1 64.2 %collective-permute-start.5 = (bf16[384,16]{0,1:T(8,128)(2,1)S(1)}, bf16[384,16]{0,1:T(8,128)(2,1)S(1)}, u32[]{:S(2)}, u32[]{:S(2)}) collective-permute-start(bf16[384,16]{0,1:T(8,128)(2,1)S(1)} %fusion.16), channel_id=1, source_target_pairs={{0,6},{1,7},{2,0},{3,1},{4,2},{5,3},{6,4},{7,5},{8,14},{9,15},{10,... | collective-permute-start | bytes 36872 | tf_op jit(solution)/shard_map/ppermute | solution.py:60
  168.1 64.2 %collective-permute-start.6 = (bf16[384,16]{0,1:T(8,128)(2,1)S(1)}, bf16[384,16]{0,1:T(8,128)(2,1)S(1)}, u32[]{:S(2)}, u32[]{:S(2)}) collective-permute-start(bf16[384,16]{0,1:T(8,128)(2,1)S(1)} %fusion.16), channel_id=1, source_target_pairs={{0,7},{1,0},{2,1},{3,2},{4,3},{5,4},{6,5},{7,6},{8,15},{9,8},{10,9... | collective-permute-start | bytes 36872 | tf_op jit(solution)/shard_map/ppermute | solution.py:60
  307.9 34.4 %copy-start.2 = (bf16[384,640]{1,0:T(8,128)(2,1)S(1)}, bf16[384,640]{1,0:T(8,128)(2,1)}, u32[]{:S(2)}) copy-start(bf16[384,640]{1,0:T(8,128)(2,1)} %fusion.13) | copy-start | bytes 1474564
Sparse Core Ops, SparseCore 0:
  9.5 57.0 all-gather.5
  73.9 36.2 reduce-scatter.2
  113.5 33.2 all-gather.11
  148.8 73.8 all-gather.7
  224.6 74.0 all-gather.9
  308.0 34.2 reduce-scatter.4
